TPU v7x, 32 devices: a whole 2x2x4 slice. The times are simulated.
32 devices in a mesh: dp: 8 (over y, x, core), tensor: 4 (over z).
Axes of the slice: x: 2, y: 2, z: 4, core: 2. Of those that a mesh axis runs over, the one named last changes fastest.
Arguments:
- inputs: bfloat16 [4096, 2048], P('dp'), may hold values from -6 to 6
- active: int32 [4096], P('dp'), may hold values from 0 to 1, as said below
- block_table: int32 [16], replicated, may hold values from 0 to 15, as said below
- gain_one: bfloat16 [2048], replicated, may hold values from 0.099609375 to 1.8984375
- w_query: bfloat16 [2048, 2048], P(None, 'tensor'), may hold values from -0.125 to 0.125
- w_key: bfloat16 [2048, 1024], P(None, 'tensor'), may hold values from -0.125 to 0.125
- w_value: bfloat16 [2048, 1024], P(None, 'tensor'), may hold values from -0.125 to 0.125
- w_out: bfloat16 [2048, 2048], P('tensor'), may hold values from -4 to 4
- gain_two: bfloat16 [2048], replicated, may hold values from 0.099609375 to 1.8984375
- w_gate: bfloat16 [2048, 5632], P(None, 'tensor'), may hold values from -0.125 to 0.125
- w_up: bfloat16 [2048, 5632], P(None, 'tensor'), may hold values from -0.125 to 0.125
- w_down: bfloat16 [5632, 2048], P('tensor'), may hold values from -0.078125 to 0.078125
- cotangent: bfloat16 [4096, 2048], P('dp'), may hold values from -6 to 6
Outputs:
- output: bfloat16 [4096, 2048], P('dp')
- grad_input: float32 [4096, 2048], P('dp')
- grad_gain_one: float32 [2048], replicated
- grad_w_query: float32 [2048, 2048], P(None, 'tensor')
- grad_w_key: float32 [2048, 1024], P(None, 'tensor')
- grad_w_value: float32 [2048, 1024], P(None, 'tensor')
- grad_w_out: float32 [2048, 2048], P('tensor')
- grad_gain_two: float32 [2048], replicated
- grad_w_gate: float32 [2048, 5632], P(None, 'tensor')
- grad_w_up: float32 [2048, 5632], P(None, 'tensor')
- grad_w_down: float32 [5632, 2048], P('tensor')
Inputs may be any that keep to these rules, and one draw needn't show every extreme that they name: `active`: 0 or 1 for every token; the share of 1s differs from one causal block to another. `block_table`: each causal block appears once; entries 2i and 2i+1 sum to 15.
All inputs are finite; a program needn't handle non-finite values.
Results may differ from a plain program's by a relative error of at most 0.014.
Values may be sent and summed in bfloat16 or wider, within the bound.
No kernel may reach another device: no remote copies, remote signals or barrier semaphores. Data moves between devices by JAX's collectives and lax.ppermute only.
A program may use at most 256 MiB of HBM per device.

v0:
```python
import jax
import jax.numpy as jnp
from jax import lax
from jax.sharding import PartitionSpec as P

HEAD_DIM = 128
EPS = 1e-05
MASKED_SCORE = -1e30


def rms_norm(values, scales):
    return values * lax.rsqrt(jnp.mean(values * values, axis=-1, keepdims=True) + EPS) * scales


def rotate(values, cos_table, sin_table):
    middle = values.shape[-1] // 2
    leading = values[..., :middle]
    trailing = values[..., middle:]
    return jnp.concatenate(
        [leading * cos_table - trailing * sin_table, trailing * cos_table + leading * sin_table],
        axis=-1,
    )


def angles_of(positions, head_size):
    frequency = 10000.0 ** (-jnp.arange(0, head_size, 2, dtype=jnp.float32) / head_size)
    angles = positions.astype(jnp.float32)[:, None] * frequency[None, :]
    return (jnp.cos(angles)[:, None, :], jnp.sin(angles)[:, None, :])


def swiglu(gate_value, up_value):
    return jax.nn.silu(gate_value) * up_value


def left_trans(left, right):
    return lax.dot_general(
        left, right, (((0,), (0,)), ((), ())), preferred_element_type=jnp.float32
    )


def right_trans(left, right):
    return lax.dot_general(
        left, right, (((1,), (1,)), ((), ())), preferred_element_type=jnp.float32
    )


def partner_perm(axis_size, mask):
    return [(index, index ^ mask) for index in range(axis_size)]


def permute_sum(parts, dims, axis):
    size = lax.axis_size(axis)
    steps = size.bit_length() - 1
    assert 1 << steps == size
    me = lax.axis_index(axis)
    pieces = list(parts)
    for step in range(steps):
        bit = me >> step & 1
        keep, send = ([], [])
        for piece, dim in zip(pieces, dims):
            half = piece.shape[dim] // 2
            keep.append(lax.dynamic_slice_in_dim(piece, bit * half, half, axis=dim))
            send.append(
                lax.dynamic_slice_in_dim(piece, (1 - bit) * half, half, axis=dim).astype(
                    jnp.bfloat16
                )
            )
        got = lax.ppermute(send, axis, partner_perm(size, 1 << step))
        pieces = [mine + theirs.astype(jnp.float32) for mine, theirs in zip(keep, got)]
    pieces = [piece.astype(jnp.bfloat16) for piece in pieces]
    for step in reversed(range(steps)):
        first = me >> step & 1 == 0
        got = lax.ppermute(pieces, axis, partner_perm(size, 1 << step))
        pieces = [
            jnp.concatenate(
                [jnp.where(first, mine, theirs), jnp.where(first, theirs, mine)], axis=dim
            )
            for mine, theirs, dim in zip(pieces, got, dims)
        ]
    return [piece.astype(jnp.float32) for piece in pieces]


def permute_allsum(value, axis):
    size = lax.axis_size(axis)
    steps = size.bit_length() - 1
    for step in range(steps):
        value = value + lax.ppermute(value, axis, partner_perm(size, 1 << step))
    return value


def on_device(
    inputs,
    active,
    block_table,
    gain_one,
    w_query,
    w_key,
    w_value,
    w_out,
    gain_two,
    w_gate,
    w_up,
    w_down,
    cotangent,
):
    row_count = inputs.shape[0]
    local_heads = w_query.shape[1] // HEAD_DIM
    local_groups = w_key.shape[1] // HEAD_DIM
    group_size = local_heads // local_groups
    half_rows = row_count // 2
    length = row_count * lax.axis_size("dp")
    score_scale = HEAD_DIM ** (-0.5)
    key_pos = (
        block_table[:, None] * half_rows + jnp.arange(half_rows, dtype=jnp.int32)[None, :]
    ).reshape(length)
    row_start = lax.axis_index("dp") * row_count
    query_pos = lax.dynamic_slice_in_dim(key_pos, row_start, row_count)
    slot_ids = jnp.arange(length, dtype=jnp.int32)
    own_ids = row_start + jnp.arange(row_count, dtype=jnp.int32)
    cos_table, sin_table = angles_of(query_pos, HEAD_DIM)
    keep_rows = active.astype(jnp.float32)[:, None]
    source = inputs.astype(jnp.float32)
    normed_full, norm_one_back = jax.vjp(rms_norm, source, gain_one.astype(jnp.float32))
    normed = normed_full.astype(jnp.bfloat16)
    query_raw = jnp.dot(normed, w_query, preferred_element_type=jnp.float32).reshape(
        row_count, local_heads, HEAD_DIM
    )
    key_raw = jnp.dot(normed, w_key, preferred_element_type=jnp.float32).reshape(
        row_count, local_groups, HEAD_DIM
    )
    value_low = jnp.dot(normed, w_value, preferred_element_type=jnp.float32).astype(jnp.bfloat16)
    query_low = (
        rotate(query_raw, cos_table, sin_table)
        .reshape(row_count, local_heads * HEAD_DIM)
        .astype(jnp.bfloat16)
    )
    key_low = (
        rotate(key_raw, cos_table, sin_table)
        .reshape(row_count, local_groups * HEAD_DIM)
        .astype(jnp.bfloat16)
    )
    alive_low = active.astype(jnp.bfloat16)

    def allowed_of(alive_all):
        return (key_pos[None, :] <= query_pos[:, None]) & (
            (alive_all[None, :] > 0) | (slot_ids[None, :] == own_ids[:, None])
        )

    def head_scores(head_index, keys_all, allowed):
        query_part = query_low[:, head_index * HEAD_DIM : (head_index + 1) * HEAD_DIM]
        group_index = head_index // group_size
        key_part = keys_all[:, group_index * HEAD_DIM : (group_index + 1) * HEAD_DIM]
        raw_scores = right_trans(query_part, key_part) * score_scale
        return jnp.where(allowed, raw_scores, MASKED_SCORE)

    kv_width = local_groups * HEAD_DIM
    all_kv = lax.all_gather(jnp.concatenate([key_low, value_low], axis=1), "dp", axis=0, tiled=True)
    all_keys = all_kv[:, :kv_width]
    all_values = all_kv[:, kv_width:]
    all_alive = lax.all_gather(alive_low, "dp", axis=0, tiled=True)
    allowed_fwd = allowed_of(all_alive)
    mixed_parts = []
    lse_parts = []
    for head_index in range(local_heads):
        masked = head_scores(head_index, all_keys, allowed_fwd)
        row_max = jnp.max(masked, axis=1, keepdims=True)
        shifted = jnp.exp(masked - row_max)
        row_total = jnp.sum(shifted, axis=1, keepdims=True)
        probs_low = (shifted / row_total).astype(jnp.bfloat16)
        lse_parts.append(row_max + jnp.log(row_total))
        group_index = head_index // group_size
        value_part = all_values[:, group_index * HEAD_DIM : (group_index + 1) * HEAD_DIM]
        mixed_parts.append(jnp.dot(probs_low, value_part, preferred_element_type=jnp.float32))
    attended = jnp.concatenate(mixed_parts, axis=1).astype(jnp.bfloat16)
    branch = lax.psum(
        jnp.dot(attended, w_out, preferred_element_type=jnp.float32).astype(jnp.bfloat16), "tensor"
    ).astype(jnp.float32)
    middle = source + keep_rows * branch
    normed_two_full, norm_two_back = jax.vjp(rms_norm, middle, gain_two.astype(jnp.float32))
    normed_two = normed_two_full.astype(jnp.bfloat16)
    gate_value = jnp.dot(normed_two, w_gate, preferred_element_type=jnp.float32)
    up_value = jnp.dot(normed_two, w_up, preferred_element_type=jnp.float32)
    hidden_full, swiglu_back = jax.vjp(swiglu, gate_value, up_value)
    hidden = hidden_full.astype(jnp.bfloat16)
    down_sum = lax.psum(
        jnp.dot(hidden, w_down, preferred_element_type=jnp.float32).astype(jnp.bfloat16), "tensor"
    ).astype(jnp.float32)
    output = (middle + keep_rows * down_sum).astype(jnp.bfloat16)
    grad_out = cotangent.astype(jnp.float32)
    d_down = (keep_rows * grad_out).astype(jnp.bfloat16)
    grad_w_down = left_trans(hidden, d_down)
    d_hidden = right_trans(d_down, w_down)
    d_gate_full, d_up_full = swiglu_back(d_hidden)
    d_gate = d_gate_full.astype(jnp.bfloat16)
    d_up = d_up_full.astype(jnp.bfloat16)
    grad_w_gate = left_trans(normed_two, d_gate)
    grad_w_up = left_trans(normed_two, d_up)
    d_normed_two = lax.psum(
        (right_trans(d_gate, w_gate) + right_trans(d_up, w_up)).astype(jnp.bfloat16), "tensor"
    ).astype(jnp.float32)
    d_middle_norm, grad_gain_two = norm_two_back(d_normed_two)
    grad_middle = grad_out + d_middle_norm
    d_branch = (keep_rows * grad_middle).astype(jnp.bfloat16)
    grad_w_out = left_trans(attended, d_branch)
    d_attended = right_trans(d_branch, w_out).astype(jnp.bfloat16)
    back_keys, back_values = (all_keys, all_values)
    allowed_back = allowed_fwd
    d_query_parts = []
    d_key_parts = [
        jnp.zeros((length, HEAD_DIM), jnp.float32) for group_index in range(local_groups)
    ]
    d_value_parts = [
        jnp.zeros((length, HEAD_DIM), jnp.float32) for group_index in range(local_groups)
    ]
    for head_index in range(local_heads):
        group_index = head_index // group_size
        masked = head_scores(head_index, back_keys, allowed_back)
        probs = jnp.where(allowed_back, jnp.exp(masked - lse_parts[head_index]), 0.0)
        probs_low = probs.astype(jnp.bfloat16)
        d_out_part = d_attended[:, head_index * HEAD_DIM : (head_index + 1) * HEAD_DIM]
        key_part = back_keys[:, group_index * HEAD_DIM : (group_index + 1) * HEAD_DIM]
        value_part = back_values[:, group_index * HEAD_DIM : (group_index + 1) * HEAD_DIM]
        query_part = query_low[:, head_index * HEAD_DIM : (head_index + 1) * HEAD_DIM]
        d_probs = right_trans(d_out_part, value_part)
        row_delta = jnp.sum(probs * d_probs, axis=1, keepdims=True)
        d_scores = (probs * (d_probs - row_delta)).astype(jnp.bfloat16)
        d_query_parts.append(
            jnp.dot(d_scores, key_part, preferred_element_type=jnp.float32) * score_scale
        )
        d_key_parts[group_index] = (
            d_key_parts[group_index] + left_trans(d_scores, query_part) * score_scale
        )
        d_value_parts[group_index] = d_value_parts[group_index] + left_trans(probs_low, d_out_part)
    d_key_all = jnp.concatenate(d_key_parts, axis=1)
    d_value_all = jnp.concatenate(d_value_parts, axis=1)
    d_kv_own = lax.psum_scatter(
        jnp.concatenate([d_key_all, d_value_all], axis=1).astype(jnp.bfloat16),
        "dp",
        scatter_dimension=0,
        tiled=True,
    ).astype(jnp.float32)
    d_key_own = d_kv_own[:, :kv_width]
    d_value_own = d_kv_own[:, kv_width:]
    d_queries = jnp.concatenate(d_query_parts, axis=1).reshape(row_count, local_heads, HEAD_DIM)
    d_query_low = (
        rotate(d_queries, cos_table, -sin_table)
        .reshape(row_count, local_heads * HEAD_DIM)
        .astype(jnp.bfloat16)
    )
    d_key_low = (
        rotate(d_key_own.reshape(row_count, local_groups, HEAD_DIM), cos_table, -sin_table)
        .reshape(row_count, local_groups * HEAD_DIM)
        .astype(jnp.bfloat16)
    )
    d_value_low = d_value_own.astype(jnp.bfloat16)
    grad_w_query = left_trans(normed, d_query_low)
    grad_w_key = left_trans(normed, d_key_low)
    grad_w_value = left_trans(normed, d_value_low)
    d_normed_part = (
        right_trans(d_query_low, w_query)
        + right_trans(d_key_low, w_key)
        + right_trans(d_value_low, w_value)
    )
    d_normed = lax.psum(d_normed_part.astype(jnp.bfloat16), "tensor").astype(jnp.float32)
    d_source_norm, grad_gain_one = norm_one_back(d_normed)
    grad_input = grad_middle + d_source_norm
    grad_gain_one = permute_allsum(grad_gain_one, "dp")
    grad_gain_two = permute_allsum(grad_gain_two, "dp")
    grad_w_gate, grad_w_up, grad_w_down = permute_sum(
        [grad_w_gate, grad_w_up, grad_w_down], [0, 0, 1], "dp"
    )
    (grad_w_out,) = permute_sum([grad_w_out], [1], "dp")
    grad_w_query, grad_w_key, grad_w_value = permute_sum(
        [grad_w_query, grad_w_key, grad_w_value], [0, 0, 0], "dp"
    )
    return (
        output,
        grad_input,
        grad_gain_one,
        grad_w_query,
        grad_w_key,
        grad_w_value,
        grad_w_out,
        grad_gain_two,
        grad_w_gate,
        grad_w_up,
        grad_w_down,
    )


def solution(mesh):
    placed = (
        P("dp", None),
        P("dp"),
        P(),
        P(),
        P(None, "tensor"),
        P(None, "tensor"),
        P(None, "tensor"),
        P("tensor", None),
        P(),
        P(None, "tensor"),
        P(None, "tensor"),
        P("tensor", None),
        P("dp", None),
    )
    return jax.shard_map(
        on_device,
        mesh=mesh,
        in_specs=placed,
        out_specs=(
            P("dp", None),
            P("dp", None),
            P(),
            P(None, "tensor"),
            P(None, "tensor"),
            P(None, "tensor"),
            P("tensor", None),
            P(),
            P(None, "tensor"),
            P(None, "tensor"),
            P("tensor", None),
        ),
        check_vma=False,
    )
```

profile of v0, /device:TPU:0, one launch (start us, length us, event | category | flops | bytes accessed | tf_op | source)
XLA Modules:
  0.0 919.7 jit_solution(16879764175254552638)
XLA Ops:
  19.7 10.9 %all-gather = bf16[8,1,512]{2,1,0:T(2,128)(2,1)S(1)} all-gather(bf16[1,1,512]{2,1,0:T(2,128)(2,1)S(1)} %reshape.237), channel_id=1, replica_groups=mesh['dp'=8,'tensor'=4] {'dp'}, dimensions={0}, use_global_device_ids=true | all-gather | bytes 9216 | tf_op jit(solution)/shard_map/all_gather | solution.py:160
  34.7 25.2 %all-gather.3.cloned.1.call-done = bf16[4096,512]{0,1:T(8,128)(2,1)} async-done(((bf16[512,512]{0,1:T(8,128)(2,1)}), bf16[4096,512]{0,1:T(8,128)(2,1)}) %all-gather.3.cloned.1.call-update) | async-done | bytes 4194320 | tf_op jit(solution)/shard_map/all_gather | solution.py:157
  86.8 7.1 fusion.38
  103.0 86.2 %all-reduce.5.cloned.1.call-done = bf16[512,2048]{1,0:T(8,128)(2,1)} async-done(((bf16[512,2048]{1,0:T(8,128)(2,1)}), bf16[512,2048]{1,0:T(8,128)(2,1)}) %all-reduce.5.cloned.1.call-update) | async-done | bytes 2097168 | tf_op jit(solution)/shard_map/psum | solution.py:175
  193.7 8.9 fusion.115
  207.5 7.5 multiply_convert_fusion.6
  237.5 7.1 dynamic-slice_convert_fusion.1
  259.5 55.2 %all-reduce.7.cloned.1.call-done = bf16[512,2048]{1,0:T(8,128)(2,1)} async-done(((bf16[512,2048]{1,0:T(8,128)(2,1)}), bf16[512,2048]{1,0:T(8,128)(2,1)}) %all-reduce.7.cloned.1.call-update) | async-done | bytes 2097168 | tf_op jit(solution)/shard_map/psum | solution.py:198
  361.8 20.2 %multiply_reduce_fusion.2 = (f32[512]{0:T(512)S(1)}, f32[512]{0:T(512)S(1)}, f32[512]{0:T(512)S(1)}, f32[512]{0:T(512)S(1)}, f32[512,4096]{1,0:T(8,128)}) fusion(f32[512,4096]{1,0:T(8,128)S(1)} %bitcast.53, f32[512]{0:T(512)S(1)} %get-tuple-element.97, s32[512]{0:T(512)S(1)} %copy-done.74, pred[4096]{0:T(1024)(128)(4,1)S(1)} %bitcast.95, ...), kind=kOutput, calls=%fused_computation.7 | convolution fusion | flops 578811904 | bytes 68329472 | tf_op jit(solution)/shard_map/dot_general | solution.py:42
  381.9 10.0 %multiply_convert_fusion = bf16[512,4096]{1,0:T(8,128)(2,1)} fusion(f32[512,4096]{1,0:T(8,128)} %fusion.46, f32[512]{0:T(512)S(1)} %get-tuple-element.18, f32[512,4096]{1,0:T(8,128)} %copy-done.10, f32[512]{0:T(512)S(1)} %get-tuple-element.95, s32[512]{0:T(512)S(1)} %copy-done.74, pred[4096]{0:T(1024)(128)(4,1)S(1)} %bitcast.96, s32[512]{0:T(512)S(1)} %copy-done.72, ...), kind=kLoop, calls=%fused_computation | loop fusion | flops 18874368 | bytes 21000192 | tf_op jit(solution)/shard_map/convert_element_type | solution.py:226
  391.9 18.2 %multiply_convert_fusion.2 = (bf16[512,4096]{1,0:T(8,128)(2,1)}, bf16[512,4096]{1,0:T(8,128)(2,1)}, bf16[512,4096]{1,0:T(8,128)(2,1)}) fusion(f32[512,4096]{1,0:T(8,128)} %get-tuple-element.94, f32[512]{0:T(512)S(1)} %get-tuple-element.15, f32[512,4096]{1,0:T(8,128)S(1)} %bitcast.53, f32[512]{0:T(512)S(1)} %get-tuple-element.97, s32[512]{0:T(512)S(1)} %copy-done.74, ...), kind=kLoop, calls=%fused_computation.6 | loop fusion | flops 39845888 | bytes 62951424 | tf_op jit(solution)/shard_map/convert_element_type | solution.py:226
  466.2 68.0 %collective-permute-done.22 = bf16[512,512]{1,0:T(8,128)(2,1)} collective-permute-done((bf16[512,512]{1,0:T(8,128)(2,1)}, bf16[512,512]{1,0:T(8,128)(2,1)}, u32[]{:S(2)}, u32[]{:S(2)}) %collective-permute-start.22) | collective-permute-done | bytes 524320 | tf_op jit(solution)/shard_map/ppermute | solution.py:68
  537.0 8.2 collective-permute-done.4
  571.7 10.6 %collective-permute-done.31 = bf16[512,1408]{1,0:T(8,128)(2,1)S(1)} collective-permute-done((bf16[512,1408]{1,0:T(8,128)(2,1)S(1)}, bf16[512,1408]{1,0:T(8,128)(2,1)S(1)}, u32[]{:S(2)}, u32[]{:S(2)}) %collective-permute-start.31) | collective-permute-done | bytes 1441824 | tf_op jit(solution)/shard_map/ppermute | solution.py:68
  584.3 9.3 %collective-permute-done.25 = bf16[512,512]{1,0:T(8,128)(2,1)S(1)} collective-permute-done((bf16[512,512]{1,0:T(8,128)(2,1)S(1)}, bf16[512,512]{1,0:T(8,128)(2,1)S(1)}, u32[]{:S(2)}, u32[]{:S(2)}) %collective-permute-start.25) | collective-permute-done | bytes 524320 | tf_op jit(solution)/shard_map/ppermute | solution.py:73
  594.0 9.3 %collective-permute-done.7 = bf16[512,512]{1,0:T(8,128)(2,1)S(1)} collective-permute-done((bf16[512,512]{1,0:T(8,128)(2,1)S(1)}, bf16[512,512]{1,0:T(8,128)(2,1)S(1)}, u32[]{:S(2)}, u32[]{:S(2)}) %collective-permute-start.7) | collective-permute-done | bytes 524320 | tf_op jit(solution)/shard_map/ppermute | solution.py:73
  606.3 11.1 %collective-permute-done.32 = bf16[256,1408]{1,0:T(8,128)(2,1)S(1)} collective-permute-done((bf16[256,1408]{1,0:T(8,128)(2,1)S(1)}, bf16[256,1408]{1,0:T(8,128)(2,1)S(1)}, u32[]{:S(2)}, u32[]{:S(2)}) %collective-permute-start.32) | collective-permute-done | bytes 720928 | tf_op jit(solution)/shard_map/ppermute | solution.py:68
  619.3 13.5 %collective-permute-done.45 = bf16[1408,256]{1,0:T(8,128)(2,1)S(1)} collective-permute-done((bf16[1408,256]{1,0:T(8,128)(2,1)S(1)}, bf16[1408,256]{1,0:T(8,128)(2,1)S(1)}, u32[]{:S(2)}, u32[]{:S(2)}) %collective-permute-start.45) | collective-permute-done | bytes 720928 | tf_op jit(solution)/shard_map/ppermute | solution.py:73
  634.8 13.5 %collective-permute-done.39 = bf16[256,1408]{1,0:T(8,128)(2,1)S(1)} collective-permute-done((bf16[256,1408]{1,0:T(8,128)(2,1)S(1)}, bf16[256,1408]{1,0:T(8,128)(2,1)S(1)}, u32[]{:S(2)}, u32[]{:S(2)}) %collective-permute-start.39) | collective-permute-done | bytes 720928 | tf_op jit(solution)/shard_map/ppermute | solution.py:73
  650.3 11.3 %collective-permute-done.33 = bf16[256,1408]{1,0:T(8,128)(2,1)S(1)} collective-permute-done((bf16[256,1408]{1,0:T(8,128)(2,1)S(1)}, bf16[256,1408]{1,0:T(8,128)(2,1)S(1)}, u32[]{:S(2)}, u32[]{:S(2)}) %collective-permute-start.33) | collective-permute-done | bytes 720928 | tf_op jit(solution)/shard_map/ppermute | solution.py:73
  672.4 26.1 %collective-permute-done.40 = bf16[512,1408]{1,0:T(8,128)(2,1)S(1)} collective-permute-done((bf16[512,1408]{1,0:T(8,128)(2,1)S(1)}, bf16[512,1408]{1,0:T(8,128)(2,1)S(1)}, u32[]{:S(2)}, u32[]{:S(2)}) %collective-permute-start.40) | collective-permute-done | bytes 1441824 | tf_op jit(solution)/shard_map/ppermute | solution.py:73
  701.0 23.3 %collective-permute-done.34 = bf16[512,1408]{1,0:T(8,128)(2,1)S(1)} collective-permute-done((bf16[512,1408]{1,0:T(8,128)(2,1)S(1)}, bf16[512,1408]{1,0:T(8,128)(2,1)S(1)}, u32[]{:S(2)}, u32[]{:S(2)}) %collective-permute-start.34) | collective-permute-done | bytes 1441824 | tf_op jit(solution)/shard_map/ppermute | solution.py:73
  785.5 6.9 broadcast_select_fusion.5
  813.3 82.8 %all-reduce.9.cloned.1.call-done = (bf16[512,2048]{1,0:T(8,128)(2,1)}, bf16[512,2048]{1,0:T(8,128)(2,1)}) async-done(((bf16[512,2048]{1,0:T(8,128)(2,1)}, bf16[512,2048]{1,0:T(8,128)(2,1)}), (bf16[512,2048]{1,0:T(8,128)(2,1)}, bf16[512,2048]{1,0:T(8,128)(2,1)})) %all-reduce.9.cloned.1.call-update) | async-done | bytes 4194320 | tf_op jit(solution)/shard_map/psum | solution.py:185
  (472 shorter events, 353.9 us)
Async XLA Ops:
  7.2 52.7 %all-gather.3.cloned.1.call-start = ((), (), s32[]{:S(2)}) async-start(), calls=%async_computation.1 | async-start | bytes 4718592 | tf_op jit(solution)/shard_map/all_gather | solution.py:157
  19.6 169.5 %all-reduce.5.cloned.1.call-start = ((), (), s32[]{:S(2)}) async-start(), calls=%async_computation.2 | async-start | bytes 4194304 | tf_op jit(solution)/shard_map/psum | solution.py:175
  102.9 211.9 %all-reduce.7.cloned.1.call-start = ((), (), s32[]{:S(2)}) async-start(), calls=%async_computation.3 | async-start | bytes 4194304 | tf_op jit(solution)/shard_map/psum | solution.py:198
  229.5 498.4 %reduce-scatter.2.cloned.1.call-start = ((), (), s32[]{:S(2)}) async-start(), calls=%async_computation.4 | async-start | bytes 4718592 | tf_op jit(solution)/shard_map/reduce_scatter | solution.py:236
  237.5 205.8 %collective-permute-start.42 = (bf16[1408,1024]{1,0:T(8,128)(2,1)}, bf16[1408,1024]{1,0:T(8,128)(2,1)}, u32[]{:S(2)}, u32[]{:S(2)}) collective-permute-start(bf16[1408,1024]{1,0:T(8,128)(2,1)} %dynamic-slice_convert_fusion), channel_id=1, source_target_pairs={{0,4},{4,0},{8,12},{12,8},{16,20},{20,16},{24,28},{28,24},{1,5},{5... | collective-permute-start | bytes 8650760 | tf_op jit(solution)/shard_map/ppermute | solution.py:68
  244.6 206.6 %collective-permute-start.36 = (bf16[1024,1408]{1,0:T(8,128)(2,1)}, bf16[1024,1408]{1,0:T(8,128)(2,1)}, u32[]{:S(2)}, u32[]{:S(2)}) collective-permute-start(bf16[1024,1408]{1,0:T(8,128)(2,1)} %dynamic-slice_convert_fusion.1), channel_id=1, source_target_pairs={{0,4},{4,0},{8,12},{12,8},{16,20},{20,16},{24,28},{28,24},{1,5},{5... | collective-permute-start | bytes 8650760 | tf_op jit(solution)/shard_map/ppermute | solution.py:68
  254.9 207.3 %collective-permute-start.30 = (bf16[1024,1408]{1,0:T(8,128)(2,1)}, bf16[1024,1408]{1,0:T(8,128)(2,1)}, u32[]{:S(2)}, u32[]{:S(2)}) collective-permute-start(bf16[1024,1408]{1,0:T(8,128)(2,1)} %dynamic-slice_convert_fusion.2), channel_id=1, source_target_pairs={{0,4},{4,0},{8,12},{12,8},{16,20},{20,16},{24,28},{28,24},{1,5},{5... | collective-permute-start | bytes 8650760 | tf_op jit(solution)/shard_map/ppermute | solution.py:68
  326.0 108.6 %collective-permute-start.27 = (f32[2048]{0:T(1024)S(1)}, f32[2048]{0:T(1024)}, u32[]{:S(2)}, u32[]{:S(2)}) collective-permute-start(f32[2048]{0:T(1024)S(1)} %get-tuple-element.11), channel_id=1, source_target_pairs={{0,4},{4,0},{8,12},{12,8},{16,20},{20,16},{24,28},{28,24},{1,5},{5... | collective-permute-start | bytes 24584 | tf_op jit(solution)/shard_map/ppermute | solution.py:87
  336.8 120.4 %collective-permute-start.21 = (bf16[512,1024]{1,0:T(8,128)(2,1)}, bf16[512,1024]{1,0:T(8,128)(2,1)}, u32[]{:S(2)}, u32[]{:S(2)}) collective-permute-start(bf16[512,1024]{1,0:T(8,128)(2,1)} %dynamic-slice_convert_fusion.6), channel_id=1, source_target_pairs={{0,4},{4,0},{8,12},{12,8},{16,20},{20,16},{24,28},{28,24},{1,5},{5... | collective-permute-start | bytes 3145736 | tf_op jit(solution)/shard_map/ppermute | solution.py:68
  420.6 475.5 %all-reduce.9.cloned.1.call-start = ((), (), s32[]{:S(2)}) async-start(), calls=%async_computation.5 | async-start | bytes 8388608 | tf_op jit(solution)/shard_map/psum | solution.py:185
  449.6 115.8 %collective-permute-start.43 = (bf16[1408,512]{1,0:T(8,128)(2,1)}, bf16[1408,512]{1,0:T(8,128)(2,1)}, u32[]{:S(2)}, u32[]{:S(2)}) collective-permute-start(bf16[1408,512]{1,0:T(8,128)(2,1)} %dynamic-slice_convert_fusion.3), channel_id=1, source_target_pairs={{0,8},{4,12},{8,0},{12,4},{16,24},{20,28},{24,16},{28,20},{1,9},{5... | collective-permute-start | bytes 4325384 | tf_op jit(solution)/shard_map/ppermute | solution.py:68
  456.7 112.5 %collective-permute-start.37 = (bf16[512,1408]{1,0:T(8,128)(2,1)}, bf16[512,1408]{1,0:T(8,128)(2,1)}, u32[]{:S(2)}, u32[]{:S(2)}) collective-permute-start(bf16[512,1408]{1,0:T(8,128)(2,1)} %dynamic-slice_convert_fusion.4), channel_id=1, source_target_pairs={{0,8},{4,12},{8,0},{12,4},{16,24},{20,28},{24,16},{28,20},{1,9},{5... | collective-permute-start | bytes 4325384 | tf_op jit(solution)/shard_map/ppermute | solution.py:68
  459.7 74.5 %collective-permute-start.22 = (bf16[512,512]{1,0:T(8,128)(2,1)}, bf16[512,512]{1,0:T(8,128)(2,1)}, u32[]{:S(2)}, u32[]{:S(2)}) collective-permute-start(bf16[512,512]{1,0:T(8,128)(2,1)} %dynamic-slice_convert_fusion.11), channel_id=1, source_target_pairs={{0,8},{4,12},{8,0},{12,4},{16,24},{20,28},{24,16},{28,20},{1,9},{5... | collective-permute-start | bytes 1572872 | tf_op jit(solution)/shard_map/ppermute | solution.py:68
  461.7 83.5 %collective-permute-start.4 = (bf16[512,512]{1,0:T(8,128)(2,1)S(1)}, bf16[512,512]{1,0:T(8,128)(2,1)S(1)}, u32[]{:S(2)}, u32[]{:S(2)}) collective-permute-start(bf16[512,512]{1,0:T(8,128)(2,1)S(1)} %dynamic-slice_convert_fusion.14), channel_id=1, source_target_pairs={{0,8},{4,12},{8,0},{12,4},{16,24},{20,28},{24,16},{28,20},{1,9},{5... | collective-permute-start | bytes 1572872 | tf_op jit(solution)/shard_map/ppermute | solution.py:68
  565.0 38.3 %collective-permute-start.7 = (bf16[512,512]{1,0:T(8,128)(2,1)S(1)}, bf16[512,512]{1,0:T(8,128)(2,1)S(1)}, u32[]{:S(2)}, u32[]{:S(2)}) collective-permute-start(bf16[512,512]{1,0:T(8,128)(2,1)S(1)} %pad_maximum_fusion.14), channel_id=1, source_target_pairs={{0,8},{4,12},{8,0},{12,4},{16,24},{20,28},{24,16},{28,20},{1,9},{5... | collective-permute-start | bytes 1572872 | tf_op jit(solution)/shard_map/ppermute | solution.py:73
  593.9 69.7 %collective-permute-start.26 = (bf16[512,1024]{1,0:T(8,128)(2,1)S(1)}, bf16[512,1024]{1,0:T(8,128)(2,1)S(1)}, u32[]{:S(2)}, u32[]{:S(2)}) collective-permute-start(bf16[512,1024]{1,0:T(8,128)(2,1)S(1)} %pad_maximum_fusion.9), channel_id=1, source_target_pairs={{0,4},{4,0},{8,12},{12,8},{16,20},{20,16},{24,28},{28,24},{1,5},{5... | collective-permute-start | bytes 3145736 | tf_op jit(solution)/shard_map/ppermute | solution.py:73
  603.6 63.1 %collective-permute-start.8 = (bf16[1024,512]{1,0:T(8,128)(2,1)S(1)}, bf16[1024,512]{1,0:T(8,128)(2,1)S(1)}, u32[]{:S(2)}, u32[]{:S(2)}) collective-permute-start(bf16[1024,512]{1,0:T(8,128)(2,1)S(1)} %pad_maximum_fusion.8), channel_id=1, source_target_pairs={{0,4},{4,0},{8,12},{12,8},{16,20},{20,16},{24,28},{28,24},{1,5},{5... | collective-permute-start | bytes 3145736 | tf_op jit(solution)/shard_map/ppermute | solution.py:73
  605.7 42.6 %collective-permute-start.39 = (bf16[256,1408]{1,0:T(8,128)(2,1)S(1)}, bf16[256,1408]{1,0:T(8,128)(2,1)S(1)}, u32[]{:S(2)}, u32[]{:S(2)}) collective-permute-start(bf16[256,1408]{1,0:T(8,128)(2,1)S(1)} %add_convert_fusion.4), channel_id=1, source_target_pairs={{0,16},{4,20},{8,24},{12,28},{16,0},{20,4},{24,8},{28,12},{1,17},{... | collective-permute-start | bytes 2162696 | tf_op jit(solution)/shard_map/ppermute | solution.py:73
  617.5 44.1 %collective-permute-start.33 = (bf16[256,1408]{1,0:T(8,128)(2,1)S(1)}, bf16[256,1408]{1,0:T(8,128)(2,1)S(1)}, u32[]{:S(2)}, u32[]{:S(2)}) collective-permute-start(bf16[256,1408]{1,0:T(8,128)(2,1)S(1)} %add_convert_fusion.5), channel_id=1, source_target_pairs={{0,16},{4,20},{8,24},{12,28},{16,0},{20,4},{24,8},{28,12},{1,17},{... | collective-permute-start | bytes 2162696 | tf_op jit(solution)/shard_map/ppermute | solution.py:73
  648.6 49.9 %collective-permute-start.40 = (bf16[512,1408]{1,0:T(8,128)(2,1)S(1)}, bf16[512,1408]{1,0:T(8,128)(2,1)S(1)}, u32[]{:S(2)}, u32[]{:S(2)}) collective-permute-start(bf16[512,1408]{1,0:T(8,128)(2,1)S(1)} %pad_maximum_fusion.5), channel_id=1, source_target_pairs={{0,8},{4,12},{8,0},{12,4},{16,24},{20,28},{24,16},{28,20},{1,9},{5... | collective-permute-start | bytes 4325384 | tf_op jit(solution)/shard_map/ppermute | solution.py:73
  661.9 62.4 %collective-permute-start.34 = (bf16[512,1408]{1,0:T(8,128)(2,1)S(1)}, bf16[512,1408]{1,0:T(8,128)(2,1)S(1)}, u32[]{:S(2)}, u32[]{:S(2)}) collective-permute-start(bf16[512,1408]{1,0:T(8,128)(2,1)S(1)} %pad_maximum_fusion.4), channel_id=1, source_target_pairs={{0,8},{4,12},{8,0},{12,4},{16,24},{20,28},{24,16},{28,20},{1,9},{5... | collective-permute-start | bytes 4325384 | tf_op jit(solution)/shard_map/ppermute | solution.py:73
  672.4 104.5 %collective-permute-start.47 = (bf16[1408,1024]{1,0:T(8,128)(2,1)}, bf16[1408,1024]{1,0:T(8,128)(2,1)}, u32[]{:S(2)}, u32[]{:S(2)}) collective-permute-start(bf16[1408,1024]{1,0:T(8,128)(2,1)} %pad_maximum_fusion.3), channel_id=1, source_target_pairs={{0,4},{4,0},{8,12},{12,8},{16,20},{20,16},{24,28},{28,24},{1,5},{5... | collective-permute-start | bytes 8650760 | tf_op jit(solution)/shard_map/ppermute | solution.py:73
  701.0 78.8 %collective-permute-start.41 = (bf16[1024,1408]{1,0:T(8,128)(2,1)}, bf16[1024,1408]{1,0:T(8,128)(2,1)}, u32[]{:S(2)}, u32[]{:S(2)}) collective-permute-start(bf16[1024,1408]{1,0:T(8,128)(2,1)} %pad_maximum_fusion.2), channel_id=1, source_target_pairs={{0,4},{4,0},{8,12},{12,8},{16,20},{20,16},{24,28},{28,24},{1,5},{5... | collective-permute-start | bytes 8650760 | tf_op jit(solution)/shard_map/ppermute | solution.py:73
  727.8 57.6 %collective-permute-start.35 = (bf16[1024,1408]{1,0:T(8,128)(2,1)}, bf16[1024,1408]{1,0:T(8,128)(2,1)}, u32[]{:S(2)}, u32[]{:S(2)}) collective-permute-start(bf16[1024,1408]{1,0:T(8,128)(2,1)} %pad_maximum_fusion.1), channel_id=1, source_target_pairs={{0,4},{4,0},{8,12},{12,8},{16,20},{20,16},{24,28},{28,24},{1,5},{5... | collective-permute-start | bytes 8650760 | tf_op jit(solution)/shard_map/ppermute | solution.py:73
  (127 other events, 1997.2 us)
Sparse Core Ops, SparseCore 0:
  19.8 40.0 all-gather.2
  103.0 86.1 all-reduce.4
  229.6 85.1 all-reduce.6
  420.7 59.7 reduce-scatter.1
  740.0 156.0 all-reduce.8
where the time goes:
time: 924 us; the launch traced here: 920 us
  waiting for transfers between devices  494 us (53%)
  matrix products  174 us (19%)
  other arithmetic  148 us (16%)
  starting transfers between devices  42.3 us (5%)
  local copies, waits for them, and re-layouts  35.2 us (4%)
  between operations  15.7 us (2%)
  blocking collectives  10.9 us (1%)
    ppermute x21, waiting for transfers between devices, permute_sum(): got = lax.ppermute(pieces, axis, partner_perm(size, 1 << step))  123 us
    ppermute x21, waiting for transfers between devices, permute_sum(): got = lax.ppermute(send, axis, partner_perm(size, 1 << step))  117 us
    psum x1, waiting for transfers between devices, on_device(): lax.psum(jnp.dot(attended, w_out, preferred_element_type=jnp.float32).ast...  86.2 us
    psum x1, waiting for transfers between devices, on_device(): lax.psum(jnp.dot(hidden, w_down, preferred_element_type=jnp.float32).asty...  82.8 us
    dot_general x15, matrix products, right_trans(): lax.dot_general(left, right, (((1,), (1,)), ((), ())), preferred_element_...  72.6 us
    psum x1, waiting for transfers between devices, on_device(): lax.psum((right_trans(d_gate, w_gate) + right_trans(d_up, w_up)).astype(j...  55.2 us
    dot_general x15, matrix products, left_trans(): lax.dot_general(left, right, (((0,), (0,)), ((), ())), preferred_element_...  45.3 us
    convert_element_type x2, other arithmetic, on_device(): d_scores = (probs * (d_probs - row_delta)).astype(jnp.bfloat16)  28.1 us
  transfers between devices with their start and end apart: 53, of which 28 were waited for; matrix products, arithmetic and copies ran while one was open for 27% of the time, Pallas kernels for 0%

commit v1 on v0

--- a/solution.py
+++ b/solution.py
@@ -195,8 +195,11 @@
     d_up = d_up_full.astype(jnp.bfloat16)
     grad_w_gate = left_trans(normed_two, d_gate)
     grad_w_up = left_trans(normed_two, d_up)
-    d_normed_two = lax.psum(
-        (right_trans(d_gate, w_gate) + right_trans(d_up, w_up)).astype(jnp.bfloat16), "tensor"
+    d_normed_two = jnp.sum(
+        lax.all_gather(
+            (right_trans(d_gate, w_gate) + right_trans(d_up, w_up)).astype(jnp.bfloat16), "tensor"
+        ),
+        axis=0,
     ).astype(jnp.float32)
     d_middle_norm, grad_gain_two = norm_two_back(d_normed_two)
     grad_middle = grad_out + d_middle_norm

time: 924 us -> 882 us (0.955)
  waiting for transfers between devices: 494 us -> 460 us
  matrix products: 174 us -> 162 us
    psum x1 -> x0, waiting for transfers between devices: 55.2 us -> none  [on_device(): lax.psum((right_trans(d_gate, w_gate) + right_trans(d_up, w_up)).astype(j...]
    psum x1, waiting for transfers between devices: 82.8 us -> 114 us  [on_device(): lax.psum(jnp.dot(hidden, w_down, preferred_element_type=jnp.float32).asty...]
    ppermute x21, waiting for transfers between devices: 123 us -> 108 us  [permute_sum(): got = lax.ppermute(pieces, axis, partner_perm(size, 1 << step))]
    unnamed x199 -> x219, local copies, waits for them, and re-layouts: 15.7 us -> 24.1 us
  transfers between devices with their start and end apart: 53 -> 53, of which waited for: 28 -> 25; matrix products, arithmetic and copies ran while one was open for 27% -> 27% of each run, Pallas kernels for 0% -> 0%
where the time goes in v1:
time: 882 us; the launch traced here: 879 us
  waiting for transfers between devices  460 us (52%)
  matrix products  162 us (18%)
  other arithmetic  148 us (17%)
  starting transfers between devices  46.1 us (5%)
  local copies, waits for them, and re-layouts  36.7 us (4%)
  between operations  16.1 us (2%)
  blocking collectives  10.6 us (1%)
    ppermute x21, waiting for transfers between devices, permute_sum(): got = lax.ppermute(send, axis, partner_perm(size, 1 << step))  125 us
    psum x1, waiting for transfers between devices, on_device(): lax.psum(jnp.dot(hidden, w_down, preferred_element_type=jnp.float32).asty...  114 us
    ppermute x21, waiting for transfers between devices, permute_sum(): got = lax.ppermute(pieces, axis, partner_perm(size, 1 << step))  108 us
    psum x1, waiting for transfers between devices, on_device(): lax.psum(jnp.dot(attended, w_out, preferred_element_type=jnp.float32).ast...  85 us
    dot_general x15, matrix products, right_trans(): lax.dot_general(left, right, (((1,), (1,)), ((), ())), preferred_element_...  73.2 us
    dot_general x15, matrix products, left_trans(): lax.dot_general(left, right, (((0,), (0,)), ((), ())), preferred_element_...  40.5 us
    convert_element_type x2, other arithmetic, on_device(): d_scores = (probs * (d_probs - row_delta)).astype(jnp.bfloat16)  29.1 us
    all_gather x1, waiting for transfers between devices, on_device(): lax.all_gather(jnp.concatenate([key_low, value_low], axis=1), 'dp', axis=...  25.4 us
  transfers between devices with their start and end apart: 53, of which 25 were waited for; matrix products, arithmetic and copies ran while one was open for 27% of the time, Pallas kernels for 0%

profile of v1, /device:TPU:0, one launch (start us, length us, event | category | flops | bytes accessed | tf_op | source)
XLA Modules:
  0.0 878.5 jit_solution(15628225776859118273)
XLA Ops:
  19.8 10.6 %all-gather.1 = bf16[8,1,512]{2,1,0:T(2,128)(2,1)S(1)} all-gather(bf16[1,1,512]{2,1,0:T(2,128)(2,1)S(1)} %reshape.238), channel_id=1, replica_groups=mesh['dp'=8,'tensor'=4] {'dp'}, dimensions={0}, use_global_device_ids=true | all-gather | bytes 9216 | tf_op jit(solution)/shard_map/all_gather | solution.py:160
  34.5 25.4 %all-gather.5.cloned.1.call-done = bf16[4096,512]{0,1:T(8,128)(2,1)} async-done(((bf16[512,512]{0,1:T(8,128)(2,1)}), bf16[4096,512]{0,1:T(8,128)(2,1)}) %all-gather.5.cloned.1.call-update) | async-done | bytes 4194320 | tf_op jit(solution)/shard_map/all_gather | solution.py:157
  87.1 7.1 fusion.38
  104.9 85.0 %all-reduce.4.cloned.1.call-done = bf16[512,2048]{1,0:T(8,128)(2,1)} async-done(((bf16[512,2048]{1,0:T(8,128)(2,1)}), bf16[512,2048]{1,0:T(8,128)(2,1)}) %all-reduce.4.cloned.1.call-update) | async-done | bytes 2097168 | tf_op jit(solution)/shard_map/psum | solution.py:175
  194.9 8.1 fusion.115
  208.0 6.8 multiply_convert_fusion.6
  269.0 21.5 %collective-permute-done.43 = bf16[1408,512]{1,0:T(8,128)(2,1)S(1)} collective-permute-done((bf16[1408,512]{1,0:T(8,128)(2,1)S(1)}, bf16[1408,512]{1,0:T(8,128)(2,1)S(1)}, u32[]{:S(2)}, u32[]{:S(2)}) %collective-permute-start.43) | collective-permute-done | bytes 1441824 | tf_op jit(solution)/shard_map/ppermute | solution.py:68
  292.6 28.8 %collective-permute-done.37 = bf16[512,1408]{1,0:T(8,128)(2,1)S(1)} collective-permute-done((bf16[512,1408]{1,0:T(8,128)(2,1)S(1)}, bf16[512,1408]{1,0:T(8,128)(2,1)S(1)}, u32[]{:S(2)}, u32[]{:S(2)}) %collective-permute-start.37) | collective-permute-done | bytes 1441824 | tf_op jit(solution)/shard_map/ppermute | solution.py:68
  323.3 28.6 %collective-permute-done.31 = bf16[512,1408]{1,0:T(8,128)(2,1)S(1)} collective-permute-done((bf16[512,1408]{1,0:T(8,128)(2,1)S(1)}, bf16[512,1408]{1,0:T(8,128)(2,1)S(1)}, u32[]{:S(2)}, u32[]{:S(2)}) %collective-permute-start.31) | collective-permute-done | bytes 1441824 | tf_op jit(solution)/shard_map/ppermute | solution.py:68
  356.3 15.2 %collective-permute-done.45 = bf16[1408,256]{1,0:T(8,128)(2,1)S(1)} collective-permute-done((bf16[1408,256]{1,0:T(8,128)(2,1)S(1)}, bf16[1408,256]{1,0:T(8,128)(2,1)S(1)}, u32[]{:S(2)}, u32[]{:S(2)}) %collective-permute-start.45) | collective-permute-done | bytes 720928 | tf_op jit(solution)/shard_map/ppermute | solution.py:73
  373.3 13.7 %collective-permute-done.32 = bf16[256,1408]{1,0:T(8,128)(2,1)S(1)} collective-permute-done((bf16[256,1408]{1,0:T(8,128)(2,1)S(1)}, bf16[256,1408]{1,0:T(8,128)(2,1)S(1)}, u32[]{:S(2)}, u32[]{:S(2)}) %collective-permute-start.32) | collective-permute-done | bytes 720928 | tf_op jit(solution)/shard_map/ppermute | solution.py:68
  388.6 13.8 %collective-permute-done.39 = bf16[256,1408]{1,0:T(8,128)(2,1)S(1)} collective-permute-done((bf16[256,1408]{1,0:T(8,128)(2,1)S(1)}, bf16[256,1408]{1,0:T(8,128)(2,1)S(1)}, u32[]{:S(2)}, u32[]{:S(2)}) %collective-permute-start.39) | collective-permute-done | bytes 720928 | tf_op jit(solution)/shard_map/ppermute | solution.py:73
  404.2 12.4 %collective-permute-done.33 = bf16[256,1408]{1,0:T(8,128)(2,1)S(1)} collective-permute-done((bf16[256,1408]{1,0:T(8,128)(2,1)S(1)}, bf16[256,1408]{1,0:T(8,128)(2,1)S(1)}, u32[]{:S(2)}, u32[]{:S(2)}) %collective-permute-start.33) | collective-permute-done | bytes 720928 | tf_op jit(solution)/shard_map/ppermute | solution.py:73
  424.5 12.7 %collective-permute-done.40 = bf16[512,1408]{1,0:T(8,128)(2,1)S(1)} collective-permute-done((bf16[512,1408]{1,0:T(8,128)(2,1)S(1)}, bf16[512,1408]{1,0:T(8,128)(2,1)S(1)}, u32[]{:S(2)}, u32[]{:S(2)}) %collective-permute-start.40) | collective-permute-done | bytes 1441824 | tf_op jit(solution)/shard_map/ppermute | solution.py:73
  439.8 25.0 %collective-permute-done.34 = bf16[512,1408]{1,0:T(8,128)(2,1)S(1)} collective-permute-done((bf16[512,1408]{1,0:T(8,128)(2,1)S(1)}, bf16[512,1408]{1,0:T(8,128)(2,1)S(1)}, u32[]{:S(2)}, u32[]{:S(2)}) %collective-permute-start.34) | collective-permute-done | bytes 1441824 | tf_op jit(solution)/shard_map/ppermute | solution.py:73
  469.0 5.9 maximum_convert_fusion.2
  474.9 7.2 reduce_sum.160
  524.9 20.9 %multiply_reduce_fusion.2 = (f32[512]{0:T(512)S(1)}, f32[512]{0:T(512)S(1)}, f32[512]{0:T(512)S(1)}, f32[512]{0:T(512)S(1)}, f32[512,4096]{1,0:T(8,128)}) fusion(f32[512,4096]{1,0:T(8,128)} %copy-done.8, f32[512]{0:T(512)S(1)} %copy-done.81, s32[512]{0:T(512)S(1)} %copy-done.78, pred[4096]{0:T(1024)(128)(4,1)S(1)} %bitcast.96, s32[512]{0:T(512)S(1)} %copy-done.76, ...), kind=kOutput, calls=%fused_computation.7 | convolution fusion | flops 578811904 | bytes 68329472 | tf_op jit(solution)/shard_map/dot_general | solution.py:42
  545.9 9.8 %multiply_convert_fusion = bf16[512,4096]{1,0:T(8,128)(2,1)} fusion(f32[512,4096]{1,0:T(8,128)} %fusion.46, f32[512]{0:T(512)S(1)} %get-tuple-element.18, f32[512,4096]{1,0:T(8,128)} %copy-done.10, f32[512]{0:T(512)S(1)} %copy-done.85, s32[512]{0:T(512)S(1)} %copy-done.78, pred[4096]{0:T(1024)(128)(4,1)S(1)} %bitcast.97, s32[512]{0:T(512)S(1)} %copy-done.76, ...), kind=kLoop, calls=%fused_computation | loop fusion | flops 18874368 | bytes 21000192 | tf_op jit(solution)/shard_map/convert_element_type | solution.py:229
  555.7 19.3 %multiply_convert_fusion.2 = (bf16[512,4096]{1,0:T(8,128)(2,1)S(1)}, bf16[512,4096]{1,0:T(8,128)(2,1)}, bf16[512,4096]{1,0:T(8,128)(2,1)}) fusion(f32[512,4096]{1,0:T(8,128)} %get-tuple-element.94, f32[512]{0:T(512)S(1)} %get-tuple-element.15, f32[512,4096]{1,0:T(8,128)} %copy-done.8, f32[512]{0:T(512)S(1)} %copy-done.81, s32[512]{0:T(512)S(1)} %copy-done.78, ...), kind=kLoop, calls=%fused_computation.6 | loop fusion | flops 39845888 | bytes 62951424 | tf_op jit(solution)/shard_map/convert_element_type | solution.py:229
  621.7 14.4 %collective-permute-done.4 = bf16[512,512]{1,0:T(8,128)(2,1)S(1)} collective-permute-done((bf16[512,512]{1,0:T(8,128)(2,1)S(1)}, bf16[512,512]{1,0:T(8,128)(2,1)S(1)}, u32[]{:S(2)}, u32[]{:S(2)}) %collective-permute-start.4) | collective-permute-done | bytes 524320 | tf_op jit(solution)/shard_map/ppermute | solution.py:68
  670.4 7.5 collective-permute-done.7
  740.2 114.4 %all-reduce.6.cloned.1.call-done = (bf16[512,2048]{1,0:T(8,128)(2,1)}, bf16[512,2048]{1,0:T(8,128)(2,1)}) async-done(((bf16[512,2048]{1,0:T(8,128)(2,1)}, bf16[512,2048]{1,0:T(8,128)(2,1)}), (bf16[512,2048]{1,0:T(8,128)(2,1)}, bf16[512,2048]{1,0:T(8,128)(2,1)})) %all-reduce.6.cloned.1.call-update) | async-done | bytes 4194320 | tf_op jit(solution)/shard_map/psum | solution.py:185
  864.8 6.2 fusion.21
  (493 shorter events, 342.1 us)
Async XLA Ops:
  7.2 52.7 %all-gather.5.cloned.1.call-start = ((), (), s32[]{:S(2)}) async-start(), calls=%async_computation.1 | async-start | bytes 4718592 | tf_op jit(solution)/shard_map/all_gather | solution.py:157
  19.7 170.3 %all-reduce.4.cloned.1.call-start = ((), (), s32[]{:S(2)}) async-start(), calls=%async_computation.2 | async-start | bytes 4194304 | tf_op jit(solution)/shard_map/psum | solution.py:175
  103.6 371.2 %all-gather.7.cloned.1.call-start = ((), (), s32[]{:S(2)}) async-start(), calls=%async_computation.4 | async-start | bytes 10485760 | tf_op jit(solution)/shard_map/all_gather | solution.py:199
  220.5 30.2 %collective-permute-start.42 = (bf16[1408,1024]{1,0:T(8,128)(2,1)}, bf16[1408,1024]{1,0:T(8,128)(2,1)}, u32[]{:S(2)}, u32[]{:S(2)}) collective-permute-start(bf16[1408,1024]{1,0:T(8,128)(2,1)} %dynamic-slice_convert_fusion), channel_id=1, source_target_pairs={{0,4},{4,0},{8,12},{12,8},{16,20},{20,16},{24,28},{28,24},{1,5},{5... | collective-permute-start | bytes 8650760 | tf_op jit(solution)/shard_map/ppermute | solution.py:68
  229.2 28.3 %collective-permute-start.36 = (bf16[1024,1408]{1,0:T(8,128)(2,1)}, bf16[1024,1408]{1,0:T(8,128)(2,1)}, u32[]{:S(2)}, u32[]{:S(2)}) collective-permute-start(bf16[1024,1408]{1,0:T(8,128)(2,1)} %dynamic-slice_convert_fusion.1), channel_id=1, source_target_pairs={{0,4},{4,0},{8,12},{12,8},{16,20},{20,16},{24,28},{28,24},{1,5},{5... | collective-permute-start | bytes 8650760 | tf_op jit(solution)/shard_map/ppermute | solution.py:68
  250.7 437.9 %reduce-scatter.2.cloned.1.call-start = ((), (), s32[]{:S(2)}) async-start(), calls=%async_computation.3 | async-start | bytes 4718592 | tf_op jit(solution)/shard_map/reduce_scatter | solution.py:239
  256.0 34.5 %collective-permute-start.43 = (bf16[1408,512]{1,0:T(8,128)(2,1)S(1)}, bf16[1408,512]{1,0:T(8,128)(2,1)S(1)}, u32[]{:S(2)}, u32[]{:S(2)}) collective-permute-start(bf16[1408,512]{1,0:T(8,128)(2,1)S(1)} %dynamic-slice_convert_fusion.3), channel_id=1, source_target_pairs={{0,8},{4,12},{8,0},{12,4},{16,24},{20,28},{24,16},{28,20},{1,9},{5... | collective-permute-start | bytes 4325384 | tf_op jit(solution)/shard_map/ppermute | solution.py:68
  262.6 58.8 %collective-permute-start.37 = (bf16[512,1408]{1,0:T(8,128)(2,1)S(1)}, bf16[512,1408]{1,0:T(8,128)(2,1)S(1)}, u32[]{:S(2)}, u32[]{:S(2)}) collective-permute-start(bf16[512,1408]{1,0:T(8,128)(2,1)S(1)} %dynamic-slice_convert_fusion.4), channel_id=1, source_target_pairs={{0,8},{4,12},{8,0},{12,4},{16,24},{20,28},{24,16},{28,20},{1,9},{5... | collective-permute-start | bytes 4325384 | tf_op jit(solution)/shard_map/ppermute | solution.py:68
  267.6 84.3 %collective-permute-start.31 = (bf16[512,1408]{1,0:T(8,128)(2,1)S(1)}, bf16[512,1408]{1,0:T(8,128)(2,1)S(1)}, u32[]{:S(2)}, u32[]{:S(2)}) collective-permute-start(bf16[512,1408]{1,0:T(8,128)(2,1)S(1)} %dynamic-slice_convert_fusion.5), channel_id=1, source_target_pairs={{0,8},{4,12},{8,0},{12,4},{16,24},{20,28},{24,16},{28,20},{1,9},{5... | collective-permute-start | bytes 4325384 | tf_op jit(solution)/shard_map/ppermute | solution.py:68
  291.1 61.1 %collective-permute-start.44 = (bf16[1408,256]{1,0:T(8,128)(2,1)S(1)}, bf16[1408,256]{1,0:T(8,128)(2,1)S(1)}, u32[]{:S(2)}, u32[]{:S(2)}) collective-permute-start(bf16[1408,256]{1,0:T(8,128)(2,1)S(1)} %dynamic-slice_convert_fusion.8), channel_id=1, source_target_pairs={{0,16},{4,20},{8,24},{12,28},{16,0},{20,4},{24,8},{28,12},{1,17},{... | collective-permute-start | bytes 2162696 | tf_op jit(solution)/shard_map/ppermute | solution.py:68
  321.7 33.0 %collective-permute-start.38 = (bf16[256,1408]{1,0:T(8,128)(2,1)S(1)}, bf16[256,1408]{1,0:T(8,128)(2,1)S(1)}, u32[]{:S(2)}, u32[]{:S(2)}) collective-permute-start(bf16[256,1408]{1,0:T(8,128)(2,1)S(1)} %dynamic-slice_convert_fusion.9), channel_id=1, source_target_pairs={{0,16},{4,20},{8,24},{12,28},{16,0},{20,4},{24,8},{28,12},{1,17},{... | collective-permute-start | bytes 2162696 | tf_op jit(solution)/shard_map/ppermute | solution.py:68
  354.0 32.9 %collective-permute-start.32 = (bf16[256,1408]{1,0:T(8,128)(2,1)S(1)}, bf16[256,1408]{1,0:T(8,128)(2,1)S(1)}, u32[]{:S(2)}, u32[]{:S(2)}) collective-permute-start(bf16[256,1408]{1,0:T(8,128)(2,1)S(1)} %dynamic-slice_convert_fusion.10), channel_id=1, source_target_pairs={{0,16},{4,20},{8,24},{12,28},{16,0},{20,4},{24,8},{28,12},{1,17},{... | collective-permute-start | bytes 2162696 | tf_op jit(solution)/shard_map/ppermute | solution.py:68
  354.8 47.6 %collective-permute-start.39 = (bf16[256,1408]{1,0:T(8,128)(2,1)S(1)}, bf16[256,1408]{1,0:T(8,128)(2,1)S(1)}, u32[]{:S(2)}, u32[]{:S(2)}) collective-permute-start(bf16[256,1408]{1,0:T(8,128)(2,1)S(1)} %add_convert_fusion.4), channel_id=1, source_target_pairs={{0,16},{4,20},{8,24},{12,28},{16,0},{20,4},{24,8},{28,12},{1,17},{... | collective-permute-start | bytes 2162696 | tf_op jit(solution)/shard_map/ppermute | solution.py:73
  371.7 45.1 %collective-permute-start.46 = (bf16[1408,512]{1,0:T(8,128)(2,1)S(1)}, bf16[1408,512]{1,0:T(8,128)(2,1)S(1)}, u32[]{:S(2)}, u32[]{:S(2)}) collective-permute-start(bf16[1408,512]{1,0:T(8,128)(2,1)S(1)} %pad_maximum_fusion.6), channel_id=1, source_target_pairs={{0,8},{4,12},{8,0},{12,4},{16,24},{20,28},{24,16},{28,20},{1,9},{5... | collective-permute-start | bytes 4325384 | tf_op jit(solution)/shard_map/ppermute | solution.py:73
  387.1 29.5 %collective-permute-start.33 = (bf16[256,1408]{1,0:T(8,128)(2,1)S(1)}, bf16[256,1408]{1,0:T(8,128)(2,1)S(1)}, u32[]{:S(2)}, u32[]{:S(2)}) collective-permute-start(bf16[256,1408]{1,0:T(8,128)(2,1)S(1)} %add_convert_fusion.5), channel_id=1, source_target_pairs={{0,16},{4,20},{8,24},{12,28},{16,0},{20,4},{24,8},{28,12},{1,17},{... | collective-permute-start | bytes 2162696 | tf_op jit(solution)/shard_map/ppermute | solution.py:73
  402.7 34.5 %collective-permute-start.40 = (bf16[512,1408]{1,0:T(8,128)(2,1)S(1)}, bf16[512,1408]{1,0:T(8,128)(2,1)S(1)}, u32[]{:S(2)}, u32[]{:S(2)}) collective-permute-start(bf16[512,1408]{1,0:T(8,128)(2,1)S(1)} %pad_maximum_fusion.5), channel_id=1, source_target_pairs={{0,8},{4,12},{8,0},{12,4},{16,24},{20,28},{24,16},{28,20},{1,9},{5... | collective-permute-start | bytes 4325384 | tf_op jit(solution)/shard_map/ppermute | solution.py:73
  417.9 49.6 %collective-permute-start.47 = (bf16[1408,1024]{1,0:T(8,128)(2,1)S(1)}, bf16[1408,1024]{1,0:T(8,128)(2,1)S(1)}, u32[]{:S(2)}, u32[]{:S(2)}) collective-permute-start(bf16[1408,1024]{1,0:T(8,128)(2,1)S(1)} %pad_maximum_fusion.3), channel_id=1, source_target_pairs={{0,4},{4,0},{8,12},{12,8},{16,20},{20,16},{24,28},{28,24},{1,5},{5... | collective-permute-start | bytes 8650760 | tf_op jit(solution)/shard_map/ppermute | solution.py:73
  418.1 46.8 %collective-permute-start.34 = (bf16[512,1408]{1,0:T(8,128)(2,1)S(1)}, bf16[512,1408]{1,0:T(8,128)(2,1)S(1)}, u32[]{:S(2)}, u32[]{:S(2)}) collective-permute-start(bf16[512,1408]{1,0:T(8,128)(2,1)S(1)} %pad_maximum_fusion.4), channel_id=1, source_target_pairs={{0,8},{4,12},{8,0},{12,4},{16,24},{20,28},{24,16},{28,20},{1,9},{5... | collective-permute-start | bytes 4325384 | tf_op jit(solution)/shard_map/ppermute | solution.py:73
  439.8 169.3 %collective-permute-start.41 = (bf16[1024,1408]{1,0:T(8,128)(2,1)}, bf16[1024,1408]{1,0:T(8,128)(2,1)}, u32[]{:S(2)}, u32[]{:S(2)}) collective-permute-start(bf16[1024,1408]{1,0:T(8,128)(2,1)} %pad_maximum_fusion.2), channel_id=1, source_target_pairs={{0,4},{4,0},{8,12},{12,8},{16,20},{20,16},{24,28},{28,24},{1,5},{5... | collective-permute-start | bytes 8650760 | tf_op jit(solution)/shard_map/ppermute | solution.py:73
  467.5 195.4 %collective-permute-start.35 = (bf16[1024,1408]{1,0:T(8,128)(2,1)}, bf16[1024,1408]{1,0:T(8,128)(2,1)}, u32[]{:S(2)}, u32[]{:S(2)}) collective-permute-start(bf16[1024,1408]{1,0:T(8,128)(2,1)} %pad_maximum_fusion.1), channel_id=1, source_target_pairs={{0,4},{4,0},{8,12},{12,8},{16,20},{20,16},{24,28},{28,24},{1,5},{5... | collective-permute-start | bytes 8650760 | tf_op jit(solution)/shard_map/ppermute | solution.py:73
  505.4 97.2 %collective-permute-start.21 = (bf16[512,1024]{1,0:T(8,128)(2,1)}, bf16[512,1024]{1,0:T(8,128)(2,1)}, u32[]{:S(2)}, u32[]{:S(2)}) collective-permute-start(bf16[512,1024]{1,0:T(8,128)(2,1)} %dynamic-slice_convert_fusion.6), channel_id=1, source_target_pairs={{0,4},{4,0},{8,12},{12,8},{16,20},{20,16},{24,28},{28,24},{1,5},{5... | collective-permute-start | bytes 3145736 | tf_op jit(solution)/shard_map/ppermute | solution.py:68
  602.6 252.0 %all-reduce.6.cloned.1.call-start = ((), (), s32[]{:S(2)}) async-start(), calls=%async_computation.5 | async-start | bytes 8388608 | tf_op jit(solution)/shard_map/psum | solution.py:185
  608.4 27.7 %collective-permute-start.4 = (bf16[512,512]{1,0:T(8,128)(2,1)S(1)}, bf16[512,512]{1,0:T(8,128)(2,1)S(1)}, u32[]{:S(2)}, u32[]{:S(2)}) collective-permute-start(bf16[512,512]{1,0:T(8,128)(2,1)S(1)} %dynamic-slice_convert_fusion.14), channel_id=1, source_target_pairs={{0,8},{4,12},{8,0},{12,4},{16,24},{20,28},{24,16},{28,20},{1,9},{5... | collective-permute-start | bytes 1572872 | tf_op jit(solution)/shard_map/ppermute | solution.py:68
  614.7 29.2 %collective-permute-start.27 = (f32[2048]{0:T(1024)S(1)}, f32[2048]{0:T(1024)S(1)}, u32[]{:S(2)}, u32[]{:S(2)}) collective-permute-start(f32[2048]{0:T(1024)S(1)} %copy-done.79), channel_id=1, source_target_pairs={{0,4},{4,0},{8,12},{12,8},{16,20},{20,16},{24,28},{28,24},{1,5},{5... | collective-permute-start | bytes 24584 | tf_op jit(solution)/shard_map/ppermute | solution.py:87
  (137 other events, 2004.7 us)
Sparse Core Ops, SparseCore 0:
  19.8 40.0 all-gather.4
  103.8 86.1 all-reduce.3
  250.8 148.7 all-gather.6
  602.7 59.0 reduce-scatter.1
  699.5 155.0 all-reduce.5
